TPU v7x, 32 devices: a whole 2x2x4 slice. The times are simulated.
32 devices in a mesh: img: 8 (over z, core), slab: 4 (over y, x).
Axes of the slice: x: 2, y: 2, z: 4, core: 2. Of those that a mesh axis runs over, the one named last changes fastest.
Arguments:
- image_masses: float32 [8, 3072, 3072], P('img', 'slab'), may hold values from 0.1 to 10
- dual_multipliers: float32 [8, 3072, 3072], P('img', 'slab'), may hold values from 0.1 to 10
- fraction_tops: int32 [8], P('img'), may hold values from 1 to 8
- banded_submatrices: bfloat16 [24, 3, 128, 128], replicated, as said below
- band_starts: int32 [24, 3], replicated, may hold values from -2 to 2, as said below
Outputs:
- barycenter: float32 [3072, 3072], P('slab')
- new_scalings: float32 [8, 3072, 3072], P('img', 'slab')
Inputs may be any that keep to these rules, and one draw needn't show every extreme that they name: `band_starts`: each row of offsets holds three consecutive numbers in increasing order; the first row is 0, 1, 2 and the last row is -2, -1, 0. `banded_submatrices`: all entries are positive.
All inputs are finite; a program needn't handle non-finite values.
Results may differ from a plain program's by a relative error of at most 0.0032.
Values may be sent and summed in bfloat16 or wider, within the bound.
No kernel may reach another device: no remote copies, remote signals or barrier semaphores. Data moves between devices by JAX's collectives and lax.ppermute only.
A program may use at most 192 MiB of HBM per device.

v0:
```python
import jax
import jax.numpy as jnp
from jax import lax
from jax.sharding import PartitionSpec as P

ITERS = 2
HALO_BLOCKS = 2


def dense_blocks(banded_submatrices, band_starts, first_row, rows, first_col, cols):
    width = banded_submatrices.shape[2]
    block_rows = lax.dynamic_slice_in_dim(banded_submatrices, first_row, rows, axis=0)
    starts = lax.dynamic_slice_in_dim(band_starts, first_row, rows, axis=0)
    total_blocks = banded_submatrices.shape[0]
    global_col = first_row + jnp.arange(rows, dtype=jnp.int32)[:, None] + starts
    in_range = (global_col >= 0) & (global_col < total_blocks)
    local_col = global_col - first_col
    matches = (
        local_col[:, :, None] == jnp.arange(cols, dtype=jnp.int32)[None, None, :]
    ) & in_range[:, :, None]
    picked = jnp.where(
        matches[:, :, :, None, None], block_rows[:, :, None], jnp.zeros((), jnp.bfloat16)
    )
    blocks = jnp.sum(picked, axis=1)
    return blocks.transpose(0, 2, 1, 3).reshape((rows * width, cols * width))


def per_device(
    image_masses, dual_multipliers, fraction_tops, banded_submatrices, band_starts, nslab
):
    width = banded_submatrices.shape[2]
    total_blocks = banded_submatrices.shape[0]
    rows = image_masses.shape[1]
    local_blocks = rows // width
    halo = HALO_BLOCKS * width
    slab = lax.axis_index("slab")
    first = slab * local_blocks
    a_full = dense_blocks(banded_submatrices, band_starts, 0, total_blocks, 0, total_blocks)
    a_local = dense_blocks(
        banded_submatrices,
        band_starts,
        first,
        local_blocks,
        first - HALO_BLOCKS,
        local_blocks + 2 * HALO_BLOCKS,
    )
    a_prev = a_local[:, :halo]
    a_mid = a_local[:, halo : halo + rows]
    a_next = a_local[:, halo + rows :]
    total_weight = lax.psum(jnp.sum(fraction_tops).astype(jnp.float32), "img")
    weight = fraction_tops.astype(jnp.float32)[0]
    up = [(i, i + 1) for i in range(nslab - 1)]
    down = [(i + 1, i) for i in range(nslab - 1)]

    def column_pass(field):
        return lax.dot_general(
            field, a_full, (((1,), (1,)), ((), ())), preferred_element_type=jnp.float32
        ).astype(jnp.bfloat16)

    def row_pass(inner):
        from_prev = lax.ppermute(inner[rows - halo :], "slab", up)
        from_next = lax.ppermute(inner[:halo], "slab", down)
        total = jnp.dot(a_mid, inner, preferred_element_type=jnp.float32)
        total = total + jnp.dot(a_prev, from_prev, preferred_element_type=jnp.float32)
        total = total + jnp.dot(a_next, from_next, preferred_element_type=jnp.float32)
        return total.astype(jnp.bfloat16)

    def apply_kernel(field):
        return row_pass(column_pass(field))

    masses = image_masses[0]
    scaling = dual_multipliers[0]
    barycenter = None
    for iteration in range(ITERS):
        kernel_v = apply_kernel(scaling.astype(jnp.bfloat16))
        scaled_u = (masses / kernel_v.astype(jnp.float32)).astype(jnp.bfloat16)
        kernel_u = apply_kernel(scaled_u).astype(jnp.float32)
        value_portion = weight * jnp.log(kernel_u)
        barycenter = jnp.exp(lax.psum(value_portion, "img") / total_weight)
        scaling = barycenter / kernel_u
    return (barycenter, scaling[None])


def solution(mesh):
    nslab = mesh.shape["slab"]
    placed = (P("img", "slab", None), P("img", "slab", None), P("img"), P(), P())

    def body(*args):
        return per_device(*args, nslab=nslab)

    return jax.shard_map(
        body,
        mesh=mesh,
        in_specs=placed,
        out_specs=(P("slab", None), P("img", "slab", None)),
        check_vma=False,
    )
```

profile of v0, /device:TPU:0, one launch (start us, length us, event | category | flops | bytes accessed | tf_op | source)
XLA Modules:
  0.0 904.0 jit_solution(9013752518304244725)
XLA Ops:
  8.9 29.6 %select_reduce_fusion = bf16[24,24,128,128]{3,2,1,0:T(8,128)(2,1)} fusion(pred[24,3,24]{2,1,0:T(4,128)(4,1)S(1)} %fusion.58, bf16[24,3,128,128]{3,2,1,0:T(8,128)(2,1)} %param.8), kind=kLoop, calls=%fused_computation | loop fusion | flops 47185920 | bytes 21235392 | tf_op jit(solution)/shard_map/reduce_sum | solution.py:24
  38.5 22.0 %copy.20 = bf16[24,128,24,128]{3,2,1,0:T(8,128)(2,1)} copy(bf16[24,128,24,128]{3,1,2,0:T(8,128)(2,1)} %bitcast.56) | data formatting | bytes 37748736 | tf_op jit(solution)/shard_map/transpose | solution.py:25
  60.5 24.9 %fusion.18 = bf16[3072,768]{1,0:T(8,128)(2,1)S(1)} fusion(bf16[384,8,24,128]{3,2,1,0:T(8,128)(2,1)} %bitcast.69, f32[1,768,3072]{2,1,0:T(8,128)} %param.6), kind=kOutput, calls=%fused_computation.31 | convolution fusion | flops 14500233216 | bytes 33030144 | tf_op jit(solution)/shard_map/dot_general | solution.py:56
  89.4 6.0 collective-permute-start
  99.9 3.2 copy.17
  105.3 8.7 fusion.42
  114.0 14.2 %collective-permute-done = bf16[256,3072]{0,1:T(8,128)(2,1)} collective-permute-done((bf16[256,3072]{0,1:T(8,128)(2,1)}, bf16[256,3072]{0,1:T(8,128)(2,1)}, u32[]{:S(2)}, u32[]{:S(2)}) %collective-permute-start) | collective-permute-done | bytes 1572896 | tf_op jit(solution)/shard_map/ppermute | solution.py:61
  128.2 6.6 fusion.56
  134.8 29.1 %collective-permute-done.1 = bf16[256,3072]{0,1:T(8,128)(2,1)} collective-permute-done((bf16[256,3072]{0,1:T(8,128)(2,1)}, bf16[256,3072]{0,1:T(8,128)(2,1)}, u32[]{:S(2)}, u32[]{:S(2)}) %collective-permute-start.1) | collective-permute-done | bytes 1572896 | tf_op jit(solution)/shard_map/ppermute | solution.py:62
  163.9 31.7 %fusion.21 = bf16[768,3072]{1,0:T(8,128)(2,1)} fusion(bf16[384,8,24,128]{3,2,1,0:T(8,128)(2,1)} %bitcast.70, f32[1,768,3072]{2,1,0:T(8,128)} %param.5, f32[768,3072]{1,0:T(8,128)} %fusion.42, f32[768,3072]{1,0:T(8,128)} %fusion.56, bf16[256,3072]{0,1:T(8,128)(2,1)} %collective-permute-done.1, bf16[768,1280]{0,1:T(8,128)(2,1)S(1)} %bitcast.59), kind=kOutput, calls=%fused_computation.32 | convolution fusion | flops 15719989248 | bytes 53870592 | tf_op jit(solution)/shard_map/dot_general | solution.py:56
  195.6 2.2 fusion.63
  197.9 3.6 collective-permute-start.2
  203.7 4.0 fusion.40
  207.7 26.5 %collective-permute-done.2 = bf16[256,3072]{1,0:T(8,128)(2,1)S(1)} collective-permute-done((bf16[256,3072]{1,0:T(8,128)(2,1)S(1)}, bf16[256,3072]{1,0:T(8,128)(2,1)S(1)}, u32[]{:S(2)}, u32[]{:S(2)}) %collective-permute-start.2) | collective-permute-done | bytes 1572896 | tf_op jit(solution)/shard_map/ppermute | solution.py:61
  235.6 33.1 %collective-permute-done.3 = bf16[256,3072]{1,0:T(8,128)(2,1)} collective-permute-done((bf16[256,3072]{1,0:T(8,128)(2,1)S(1)}, bf16[256,3072]{1,0:T(8,128)(2,1)}, u32[]{:S(2)}, u32[]{:S(2)}) %collective-permute-start.3) | collective-permute-done | bytes 1572896 | tf_op jit(solution)/shard_map/ppermute | solution.py:62
  268.7 8.0 fusion.12
  276.8 16.7 %psum.22 = f32[]{:T(128)} all-reduce(f32[]{:T(128)} %bitcast), channel_id=1, replica_groups=mesh['img'=8,'slab'=4] {'img'}, use_global_device_ids=true, to_apply=%region_3.4 | all-reduce | flops 1 | bytes 8 | tf_op jit(solution)/shard_map/psum | solution.py:50
  293.5 178.1 %all-reduce.3.cloned.1.call-done = f32[768,3072]{1,0:T(8,128)} async-done(((f32[768,3072]{1,0:T(8,128)}), f32[768,3072]{1,0:T(8,128)}) %all-reduce.3.cloned.1.call-update) | async-done | bytes 9437200 | tf_op jit(solution)/shard_map/psum | solution.py:79
  471.6 24.1 %fusion.24 = bf16[768,3072]{1,0:T(8,128)(2,1)} fusion(bf16[384,8,24,128]{3,2,1,0:T(8,128)(2,1)} %bitcast.71, bf16[768,3072]{1,0:T(8,128)(2,1)} %get-tuple-element.13, f32[768,3072]{1,0:T(8,128)} %all-reduce.3.cloned.1.call-done, f32[]{:T(128)} %psum.22), kind=kOutput, calls=%fused_computation.33 | convolution fusion | flops 14507311104 | bytes 37748740 | tf_op jit(solution)/shard_map/dot_general | solution.py:56
  498.0 3.6 collective-permute-start.4
  503.2 6.3 fusion.38
  509.5 25.5 %collective-permute-done.4 = bf16[256,3072]{1,0:T(8,128)(2,1)S(1)} collective-permute-done((bf16[256,3072]{1,0:T(8,128)(2,1)S(1)}, bf16[256,3072]{1,0:T(8,128)(2,1)S(1)}, u32[]{:S(2)}, u32[]{:S(2)}) %collective-permute-start.4) | collective-permute-done | bytes 1572896 | tf_op jit(solution)/shard_map/ppermute | solution.py:61
  535.0 5.2 fusion.52
  540.1 30.6 %collective-permute-done.5 = bf16[256,3072]{1,0:T(8,128)(2,1)} collective-permute-done((bf16[256,3072]{1,0:T(8,128)(2,1)S(1)}, bf16[256,3072]{1,0:T(8,128)(2,1)}, u32[]{:S(2)}, u32[]{:S(2)}) %collective-permute-start.5) | collective-permute-done | bytes 1572896 | tf_op jit(solution)/shard_map/ppermute | solution.py:62
  570.7 37.2 %fusion.27 = bf16[768,3072]{1,0:T(8,128)(2,1)} fusion(bf16[384,8,24,128]{3,2,1,0:T(8,128)(2,1)} %bitcast.72, f32[1,768,3072]{2,1,0:T(8,128)} %param.5, f32[768,3072]{1,0:T(8,128)} %fusion.38, f32[768,3072]{1,0:T(8,128)} %fusion.52, bf16[256,3072]{1,0:T(8,128)(2,1)} %collective-permute-done.5, bf16[768,1280]{0,1:T(8,128)(2,1)S(1)} %bitcast.65), kind=kOutput, calls=%fused_computation.34 | convolution fusion | flops 15719989248 | bytes 53870592 | tf_op jit(solution)/shard_map/dot_general | solution.py:56
  610.1 3.6 collective-permute-start.6
  615.3 4.0 fusion.36
  619.3 26.9 %collective-permute-done.6 = bf16[256,3072]{1,0:T(8,128)(2,1)S(1)} collective-permute-done((bf16[256,3072]{1,0:T(8,128)(2,1)S(1)}, bf16[256,3072]{1,0:T(8,128)(2,1)S(1)}, u32[]{:S(2)}, u32[]{:S(2)}) %collective-permute-start.6) | collective-permute-done | bytes 1572896 | tf_op jit(solution)/shard_map/ppermute | solution.py:61
  647.6 33.1 %collective-permute-done.7 = bf16[256,3072]{1,0:T(8,128)(2,1)} collective-permute-done((bf16[256,3072]{1,0:T(8,128)(2,1)S(1)}, bf16[256,3072]{1,0:T(8,128)(2,1)}, u32[]{:S(2)}, u32[]{:S(2)}) %collective-permute-start.7) | collective-permute-done | bytes 1572896 | tf_op jit(solution)/shard_map/ppermute | solution.py:62
  680.8 8.0 fusion.14
  688.8 194.5 %all-reduce.5.cloned.1.call-done = f32[768,3072]{1,0:T(8,128)} async-done(((f32[768,3072]{1,0:T(8,128)}), f32[768,3072]{1,0:T(8,128)}) %all-reduce.5.cloned.1.call-update) | async-done | bytes 9437200 | tf_op jit(solution)/shard_map/psum | solution.py:79
  883.3 13.4 %fusion.15 = (f32[1,768,3072]{2,1,0:T(8,128)}, f32[768,3072]{1,0:T(8,128)}) fusion(bf16[768,3072]{1,0:T(8,128)(2,1)} %get-tuple-element.15, f32[768,3072]{1,0:T(8,128)} %all-reduce.5.cloned.1.call-done, f32[]{:T(128)} %psum.22), kind=kLoop, calls=%fused_computation.20 | loop fusion | flops 7077888 | bytes 33030148 | tf_op jit(solution)/shard_map/broadcast_in_dim | solution.py:81
  (37 shorter events, 24.3 us)
Async XLA Ops:
  7.2 464.5 %all-reduce.3.cloned.1.call-start = ((), (), s32[]{:S(2)}) async-start(), calls=%async_computation | async-start | bytes 18874368 | tf_op jit(solution)/shard_map/psum | solution.py:79
  85.4 2.2 copy-start.3
  85.4 11.6 %copy-start.4 = (s32[24,3]{0,1:T(4,128)S(1)}, s32[24,3]{0,1:T(4,128)}, u32[]{:S(2)}) copy-start(s32[24,3]{0,1:T(4,128)} %param.9) | copy-start | bytes 868
  89.4 38.8 %collective-permute-start = (bf16[256,3072]{0,1:T(8,128)(2,1)}, bf16[256,3072]{0,1:T(8,128)(2,1)}, u32[]{:S(2)}, u32[]{:S(2)}) collective-permute-start(bf16[256,3072]{0,1:T(8,128)(2,1)} %get-tuple-element.11), channel_id=1, source_target_pairs={{0,1},{1,2},{2,3},{4,5},{5,6},{6,7},{8,9},{9,10},{10,11},{12,13},{... | collective-permute-start | bytes 4718600 | tf_op jit(solution)/shard_map/ppermute | solution.py:61
  95.5 68.4 %collective-permute-start.1 = (bf16[256,3072]{0,1:T(8,128)(2,1)}, bf16[256,3072]{0,1:T(8,128)(2,1)}, u32[]{:S(2)}, u32[]{:S(2)}) collective-permute-start(bf16[256,3072]{0,1:T(8,128)(2,1)} %get-tuple-element.10), channel_id=1, source_target_pairs={{1,0},{2,1},{3,2},{5,4},{6,5},{7,6},{9,8},{10,9},{11,10},{13,12},{... | collective-permute-start | bytes 4718600 | tf_op jit(solution)/shard_map/ppermute | solution.py:62
  195.6 8.0 copy-start
  197.9 36.3 %collective-permute-start.2 = (bf16[256,3072]{1,0:T(8,128)(2,1)S(1)}, bf16[256,3072]{1,0:T(8,128)(2,1)S(1)}, u32[]{:S(2)}, u32[]{:S(2)}) collective-permute-start(bf16[256,3072]{1,0:T(8,128)(2,1)S(1)} %get-tuple-element.9), channel_id=1, source_target_pairs={{0,1},{1,2},{2,3},{4,5},{5,6},{6,7},{8,9},{9,10},{10,11},{12,13},{... | collective-permute-start | bytes 4718600 | tf_op jit(solution)/shard_map/ppermute | solution.py:61
  201.5 67.2 %collective-permute-start.3 = (bf16[256,3072]{1,0:T(8,128)(2,1)S(1)}, bf16[256,3072]{1,0:T(8,128)(2,1)}, u32[]{:S(2)}, u32[]{:S(2)}) collective-permute-start(bf16[256,3072]{1,0:T(8,128)(2,1)S(1)} %get-tuple-element.8), channel_id=1, source_target_pairs={{1,0},{2,1},{3,2},{5,4},{6,5},{7,6},{9,8},{10,9},{11,10},{13,12},{... | collective-permute-start | bytes 4718600 | tf_op jit(solution)/shard_map/ppermute | solution.py:62
  276.8 606.5 %all-reduce.5.cloned.1.call-start = ((), (), s32[]{:S(2)}) async-start(), calls=%async_computation.1 | async-start | bytes 18874368 | tf_op jit(solution)/shard_map/psum | solution.py:79
  495.8 7.4 copy-start.2
  498.0 37.0 %collective-permute-start.4 = (bf16[256,3072]{1,0:T(8,128)(2,1)S(1)}, bf16[256,3072]{1,0:T(8,128)(2,1)S(1)}, u32[]{:S(2)}, u32[]{:S(2)}) collective-permute-start(bf16[256,3072]{1,0:T(8,128)(2,1)S(1)} %get-tuple-element.7), channel_id=1, source_target_pairs={{0,1},{1,2},{2,3},{4,5},{5,6},{6,7},{8,9},{9,10},{10,11},{12,13},{... | collective-permute-start | bytes 4718600 | tf_op jit(solution)/shard_map/ppermute | solution.py:61
  501.6 69.1 %collective-permute-start.5 = (bf16[256,3072]{1,0:T(8,128)(2,1)S(1)}, bf16[256,3072]{1,0:T(8,128)(2,1)}, u32[]{:S(2)}, u32[]{:S(2)}) collective-permute-start(bf16[256,3072]{1,0:T(8,128)(2,1)S(1)} %get-tuple-element.6), channel_id=1, source_target_pairs={{1,0},{2,1},{3,2},{5,4},{6,5},{7,6},{9,8},{10,9},{11,10},{13,12},{... | collective-permute-start | bytes 4718600 | tf_op jit(solution)/shard_map/ppermute | solution.py:62
  607.9 7.4 copy-start.1
  610.1 36.1 %collective-permute-start.6 = (bf16[256,3072]{1,0:T(8,128)(2,1)S(1)}, bf16[256,3072]{1,0:T(8,128)(2,1)S(1)}, u32[]{:S(2)}, u32[]{:S(2)}) collective-permute-start(bf16[256,3072]{1,0:T(8,128)(2,1)S(1)} %get-tuple-element.5), channel_id=1, source_target_pairs={{0,1},{1,2},{2,3},{4,5},{5,6},{6,7},{8,9},{9,10},{10,11},{12,13},{... | collective-permute-start | bytes 4718600 | tf_op jit(solution)/shard_map/ppermute | solution.py:61
  613.7 67.1 %collective-permute-start.7 = (bf16[256,3072]{1,0:T(8,128)(2,1)S(1)}, bf16[256,3072]{1,0:T(8,128)(2,1)}, u32[]{:S(2)}, u32[]{:S(2)}) collective-permute-start(bf16[256,3072]{1,0:T(8,128)(2,1)S(1)} %get-tuple-element.4), channel_id=1, source_target_pairs={{1,0},{2,1},{3,2},{5,4},{6,5},{7,6},{9,8},{10,9},{11,10},{13,12},{... | collective-permute-start | bytes 4718600 | tf_op jit(solution)/shard_map/ppermute | solution.py:62
Sparse Core Ops, SparseCore 0:
  276.9 194.6 all-reduce.2
  688.9 194.3 all-reduce.4
where the time goes:
time: 908 us; the launch traced here: 904 us
  waiting for transfers between devices  591 us (65%)
  matrix products  172 us (19%)
  other arithmetic  46.1 us (5%)
  local copies, waits for them, and re-layouts  39.6 us (4%)
  starting transfers between devices  23 us (3%)
  blocking collectives  16.7 us (2%)
  between operations  15.4 us (2%)
    psum x2, waiting for transfers between devices, per_device(): barycenter = jnp.exp(lax.psum(value_portion, 'img') / total_weight)  373 us
    ppermute x4, waiting for transfers between devices, row_pass(): from_next = lax.ppermute(inner[:halo], 'slab', down)  126 us
    dot_general x4, matrix products, column_pass(): lax.dot_general(field, a_full, (((1,), (1,)), ((), ())), preferred_elemen...  118 us
    ppermute x4, waiting for transfers between devices, row_pass(): from_prev = lax.ppermute(inner[rows - halo:], 'slab', up)  93 us
    reduce_sum x2, other arithmetic, dense_blocks(): blocks = jnp.sum(picked, axis=1)  31 us
    transpose x2, local copies, waits for them, and re-layouts, dense_blocks(): return blocks.transpose(0, 2, 1, 3).reshape((rows * width, cols * width))  25.2 us
    dot_general x4, matrix products, row_pass(): total = jnp.dot(a_mid, inner, preferred_element_type=jnp.float32)  23.1 us
  transfers between devices with their start and end apart: 10, of which 10 were waited for; matrix products, arithmetic and copies ran while one was open for 5% of the time, Pallas kernels for 0%

commit v1 on v0

--- a/solution.py
+++ b/solution.py
@@ -76,7 +76,7 @@
         scaled_u = (masses / kernel_v.astype(jnp.float32)).astype(jnp.bfloat16)
         kernel_u = apply_kernel(scaled_u).astype(jnp.float32)
         value_portion = weight * jnp.log(kernel_u)
-        barycenter = jnp.exp(lax.psum(value_portion, "img") / total_weight)
+        barycenter = jnp.exp(jnp.sum(lax.all_gather(value_portion, "img"), axis=0) / total_weight)
         scaling = barycenter / kernel_u
     return (barycenter, scaling[None])
 

time: 908 us -> 1840 us (2.03)
  waiting for transfers between devices: 591 us -> 1470 us
  other arithmetic: 46.1 us -> 101 us
    all_gather x0 -> x2, waiting for transfers between devices: none -> 1250 us  [per_device(): lax.all_gather(value_portion, 'img')]
    psum x2 -> x0, waiting for transfers between devices: 373 us -> none  [per_device(): barycenter = jnp.exp(lax.psum(value_portion, 'img') / total_weight)]
    reduce_sum x0 -> x2, other arithmetic: none -> 55.4 us  [per_device(): jnp.sum(lax.all_gather(value_portion, 'img'), axis=0) / total_weight]
  transfers between devices with their start and end apart: 10 -> 10, of which waited for: 10 -> 10; matrix products, arithmetic and copies ran while one was open for 5% -> 3% of each run, Pallas kernels for 0% -> 0%
where the time goes in v1:
time: 1840 us
  waiting for transfers between devices  1470 us (80%)
  matrix products  172 us (9%)
  other arithmetic  101 us (5%)
  local copies, waits for them, and re-layouts  39.5 us (2%)
  starting transfers between devices  23.1 us (1%)
    all_gather x2, waiting for transfers between devices, per_device(): lax.all_gather(value_portion, 'img')  1250 us
    ppermute x4, waiting for transfers between devices, row_pass(): from_next = lax.ppermute(inner[:halo], 'slab', down)  126 us
    dot_general x4, matrix products, column_pass(): lax.dot_general(field, a_full, (((1,), (1,)), ((), ())), preferred_elemen...  118 us
    ppermute x4, waiting for transfers between devices, row_pass(): from_prev = lax.ppermute(inner[rows - halo:], 'slab', up)  94.2 us
    reduce_sum x2, other arithmetic, per_device(): jnp.sum(lax.all_gather(value_portion, 'img'), axis=0) / total_weight  55.4 us
  transfers between devices with their start and end apart: 10, of which 10 were waited for; matrix products, arithmetic and copies ran while one was open for 3% of the time, Pallas kernels for 0%

profile of v1, /device:TPU:0, one launch (start us, length us, event | category | flops | bytes accessed | tf_op | source)
XLA Modules:
  0.0 1835.6 jit_solution(17918362743572392295)
XLA Ops:
  8.9 29.6 %select_reduce_fusion = bf16[24,24,128,128]{3,2,1,0:T(8,128)(2,1)} fusion(pred[24,3,24]{2,1,0:T(4,128)(4,1)S(1)} %fusion.58, bf16[24,3,128,128]{3,2,1,0:T(8,128)(2,1)} %param.8), kind=kLoop, calls=%fused_computation | loop fusion | flops 47185920 | bytes 21235392 | tf_op jit(solution)/shard_map/reduce_sum | solution.py:24
  38.5 21.9 %copy.20 = bf16[24,128,24,128]{3,2,1,0:T(8,128)(2,1)} copy(bf16[24,128,24,128]{3,1,2,0:T(8,128)(2,1)} %bitcast.58) | data formatting | bytes 37748736 | tf_op jit(solution)/shard_map/transpose | solution.py:25
  60.4 24.9 %fusion.18 = bf16[3072,768]{1,0:T(8,128)(2,1)S(1)} fusion(bf16[384,8,24,128]{3,2,1,0:T(8,128)(2,1)} %bitcast.71, f32[1,768,3072]{2,1,0:T(8,128)} %param.6), kind=kOutput, calls=%fused_computation.31 | convolution fusion | flops 14500233216 | bytes 33030144 | tf_op jit(solution)/shard_map/dot_general | solution.py:56
  89.3 6.0 collective-permute-start
  105.1 8.7 fusion.42
  113.9 14.3 collective-permute-done
  128.1 6.6 fusion.56
  134.7 29.1 %collective-permute-done.1 = bf16[256,3072]{0,1:T(8,128)(2,1)} collective-permute-done((bf16[256,3072]{0,1:T(8,128)(2,1)}, bf16[256,3072]{0,1:T(8,128)(2,1)}, u32[]{:S(2)}, u32[]{:S(2)}) %collective-permute-start.1) | collective-permute-done | bytes 1572896 | tf_op jit(solution)/shard_map/ppermute | solution.py:62
  163.8 31.6 %fusion.21 = bf16[768,3072]{1,0:T(8,128)(2,1)} fusion(bf16[384,8,24,128]{3,2,1,0:T(8,128)(2,1)} %bitcast.72, f32[1,768,3072]{2,1,0:T(8,128)} %param.5, f32[768,3072]{1,0:T(8,128)} %fusion.42, f32[768,3072]{1,0:T(8,128)} %fusion.56, bf16[256,3072]{0,1:T(8,128)(2,1)} %collective-permute-done.1, bf16[768,1280]{0,1:T(8,128)(2,1)S(1)} %bitcast.61), kind=kOutput, calls=%fused_computation.32 | convolution fusion | flops 15719989248 | bytes 53870592 | tf_op jit(solution)/shard_map/dot_general | solution.py:56
  197.6 3.6 collective-permute-start.2
  203.4 4.0 fusion.40
  207.5 26.5 %collective-permute-done.2 = bf16[256,3072]{1,0:T(8,128)(2,1)S(1)} collective-permute-done((bf16[256,3072]{1,0:T(8,128)(2,1)S(1)}, bf16[256,3072]{1,0:T(8,128)(2,1)S(1)}, u32[]{:S(2)}, u32[]{:S(2)}) %collective-permute-start.2) | collective-permute-done | bytes 1572896 | tf_op jit(solution)/shard_map/ppermute | solution.py:61
  235.4 33.1 %collective-permute-done.3 = bf16[256,3072]{1,0:T(8,128)(2,1)} collective-permute-done((bf16[256,3072]{1,0:T(8,128)(2,1)S(1)}, bf16[256,3072]{1,0:T(8,128)(2,1)}, u32[]{:S(2)}, u32[]{:S(2)}) %collective-permute-start.3) | collective-permute-done | bytes 1572896 | tf_op jit(solution)/shard_map/ppermute | solution.py:62
  268.5 8.0 fusion.12
  276.6 16.5 psum.7
  293.1 617.2 %all-gather.5.cloned.1.call-done = f32[6144,3072]{1,0:T(8,128)} async-done(((f32[768,3072]{1,0:T(8,128)}), f32[6144,3072]{1,0:T(8,128)}) %all-gather.5.cloned.1.call-update) | async-done | bytes 75497488 | tf_op jit(solution)/shard_map/all_gather | solution.py:79
  910.3 27.7 %reduce_sum.48 = f32[768,3072]{1,0:T(8,128)} reduce(f32[8,768,3072]{2,1,0:T(8,128)} %bitcast.6, f32[]{:T(128)} %constant.5.clone.1), dimensions={0}, to_apply=%region_2.3 | reduce | flops 16515072 | bytes 84934656 | tf_op jit(solution)/shard_map/reduce_sum | solution.py:79
  938.0 24.0 %fusion.24 = bf16[768,3072]{1,0:T(8,128)(2,1)} fusion(bf16[384,8,24,128]{3,2,1,0:T(8,128)(2,1)} %bitcast.73, bf16[768,3072]{1,0:T(8,128)(2,1)} %get-tuple-element.13, f32[768,3072]{1,0:T(8,128)} %reduce_sum.48, f32[]{:T(128)} %psum.7), kind=kOutput, calls=%fused_computation.33 | convolution fusion | flops 14507311104 | bytes 37748740 | tf_op jit(solution)/shard_map/dot_general | solution.py:56
  964.3 3.6 collective-permute-start.4
  969.7 6.3 fusion.38
  976.0 25.8 %collective-permute-done.4 = bf16[256,3072]{1,0:T(8,128)(2,1)S(1)} collective-permute-done((bf16[256,3072]{1,0:T(8,128)(2,1)S(1)}, bf16[256,3072]{1,0:T(8,128)(2,1)S(1)}, u32[]{:S(2)}, u32[]{:S(2)}) %collective-permute-start.4) | collective-permute-done | bytes 1572896 | tf_op jit(solution)/shard_map/ppermute | solution.py:61
  1001.9 5.2 fusion.52
  1007.0 30.6 %collective-permute-done.5 = bf16[256,3072]{1,0:T(8,128)(2,1)} collective-permute-done((bf16[256,3072]{1,0:T(8,128)(2,1)S(1)}, bf16[256,3072]{1,0:T(8,128)(2,1)}, u32[]{:S(2)}, u32[]{:S(2)}) %collective-permute-start.5) | collective-permute-done | bytes 1572896 | tf_op jit(solution)/shard_map/ppermute | solution.py:62
  1037.6 37.2 %fusion.27 = bf16[768,3072]{1,0:T(8,128)(2,1)} fusion(bf16[384,8,24,128]{3,2,1,0:T(8,128)(2,1)} %bitcast.74, f32[1,768,3072]{2,1,0:T(8,128)} %param.5, f32[768,3072]{1,0:T(8,128)} %fusion.38, f32[768,3072]{1,0:T(8,128)} %fusion.52, bf16[256,3072]{1,0:T(8,128)(2,1)} %collective-permute-done.5, bf16[768,1280]{0,1:T(8,128)(2,1)S(1)} %bitcast.67), kind=kOutput, calls=%fused_computation.34 | convolution fusion | flops 15719989248 | bytes 53870592 | tf_op jit(solution)/shard_map/dot_general | solution.py:56
  1077.0 3.6 collective-permute-start.6
  1082.1 4.0 fusion.36
  1086.1 27.7 %collective-permute-done.6 = bf16[256,3072]{1,0:T(8,128)(2,1)S(1)} collective-permute-done((bf16[256,3072]{1,0:T(8,128)(2,1)S(1)}, bf16[256,3072]{1,0:T(8,128)(2,1)S(1)}, u32[]{:S(2)}, u32[]{:S(2)}) %collective-permute-start.6) | collective-permute-done | bytes 1572896 | tf_op jit(solution)/shard_map/ppermute | solution.py:61
  1115.2 33.1 %collective-permute-done.7 = bf16[256,3072]{1,0:T(8,128)(2,1)} collective-permute-done((bf16[256,3072]{1,0:T(8,128)(2,1)S(1)}, bf16[256,3072]{1,0:T(8,128)(2,1)}, u32[]{:S(2)}, u32[]{:S(2)}) %collective-permute-start.7) | collective-permute-done | bytes 1572896 | tf_op jit(solution)/shard_map/ppermute | solution.py:62
  1148.4 8.0 fusion.14
  1156.4 631.1 %all-gather.7.cloned.1.call-done = f32[6144,3072]{1,0:T(8,128)} async-done(((f32[768,3072]{1,0:T(8,128)}), f32[6144,3072]{1,0:T(8,128)}) %all-gather.7.cloned.1.call-update) | async-done | bytes 75497488 | tf_op jit(solution)/shard_map/all_gather | solution.py:79
  1787.5 27.7 %reduce_sum.49 = f32[768,3072]{1,0:T(8,128)} reduce(f32[8,768,3072]{2,1,0:T(8,128)} %bitcast.7, f32[]{:T(128)} %constant.5.clone.1), dimensions={0}, to_apply=%region_4.5 | reduce | flops 16515072 | bytes 84934656 | tf_op jit(solution)/shard_map/reduce_sum | solution.py:79
  1815.2 13.3 fusion.15
  (39 shorter events, 29.8 us)
Async XLA Ops:
  7.2 903.1 %all-gather.5.cloned.1.call-start = ((), (), s32[]{:S(2)}) async-start(), calls=%async_computation | async-start | bytes 84934656 | tf_op jit(solution)/shard_map/all_gather | solution.py:79
  85.3 2.2 copy-start.3
  85.3 11.5 copy-start.4
  89.3 38.8 %collective-permute-start = (bf16[256,3072]{0,1:T(8,128)(2,1)}, bf16[256,3072]{0,1:T(8,128)(2,1)}, u32[]{:S(2)}, u32[]{:S(2)}) collective-permute-start(bf16[256,3072]{0,1:T(8,128)(2,1)} %get-tuple-element.11), channel_id=1, source_target_pairs={{0,1},{1,2},{2,3},{4,5},{5,6},{6,7},{8,9},{9,10},{10,11},{12,13},{... | collective-permute-start | bytes 4718600 | tf_op jit(solution)/shard_map/ppermute | solution.py:61
  95.3 68.5 %collective-permute-start.1 = (bf16[256,3072]{0,1:T(8,128)(2,1)}, bf16[256,3072]{0,1:T(8,128)(2,1)}, u32[]{:S(2)}, u32[]{:S(2)}) collective-permute-start(bf16[256,3072]{0,1:T(8,128)(2,1)} %get-tuple-element.10), channel_id=1, source_target_pairs={{1,0},{2,1},{3,2},{5,4},{6,5},{7,6},{9,8},{10,9},{11,10},{13,12},{... | collective-permute-start | bytes 4718600 | tf_op jit(solution)/shard_map/ppermute | solution.py:62
  195.4 8.0 copy-start
  197.6 36.3 %collective-permute-start.2 = (bf16[256,3072]{1,0:T(8,128)(2,1)S(1)}, bf16[256,3072]{1,0:T(8,128)(2,1)S(1)}, u32[]{:S(2)}, u32[]{:S(2)}) collective-permute-start(bf16[256,3072]{1,0:T(8,128)(2,1)S(1)} %get-tuple-element.9), channel_id=1, source_target_pairs={{0,1},{1,2},{2,3},{4,5},{5,6},{6,7},{8,9},{9,10},{10,11},{12,13},{... | collective-permute-start | bytes 4718600 | tf_op jit(solution)/shard_map/ppermute | solution.py:61
  201.3 67.2 %collective-permute-start.3 = (bf16[256,3072]{1,0:T(8,128)(2,1)S(1)}, bf16[256,3072]{1,0:T(8,128)(2,1)}, u32[]{:S(2)}, u32[]{:S(2)}) collective-permute-start(bf16[256,3072]{1,0:T(8,128)(2,1)S(1)} %get-tuple-element.8), channel_id=1, source_target_pairs={{1,0},{2,1},{3,2},{5,4},{6,5},{7,6},{9,8},{10,9},{11,10},{13,12},{... | collective-permute-start | bytes 4718600 | tf_op jit(solution)/shard_map/ppermute | solution.py:62
  276.5 1511.0 %all-gather.7.cloned.1.call-start = ((), (), s32[]{:S(2)}) async-start(), calls=%async_computation.1 | async-start | bytes 84934656 | tf_op jit(solution)/shard_map/all_gather | solution.py:79
  962.1 7.6 copy-start.2
  964.3 37.6 %collective-permute-start.4 = (bf16[256,3072]{1,0:T(8,128)(2,1)S(1)}, bf16[256,3072]{1,0:T(8,128)(2,1)S(1)}, u32[]{:S(2)}, u32[]{:S(2)}) collective-permute-start(bf16[256,3072]{1,0:T(8,128)(2,1)S(1)} %get-tuple-element.7), channel_id=1, source_target_pairs={{0,1},{1,2},{2,3},{4,5},{5,6},{6,7},{8,9},{9,10},{10,11},{12,13},{... | collective-permute-start | bytes 4718600 | tf_op jit(solution)/shard_map/ppermute | solution.py:61
  967.9 69.7 %collective-permute-start.5 = (bf16[256,3072]{1,0:T(8,128)(2,1)S(1)}, bf16[256,3072]{1,0:T(8,128)(2,1)}, u32[]{:S(2)}, u32[]{:S(2)}) collective-permute-start(bf16[256,3072]{1,0:T(8,128)(2,1)S(1)} %get-tuple-element.6), channel_id=1, source_target_pairs={{1,0},{2,1},{3,2},{5,4},{6,5},{7,6},{9,8},{10,9},{11,10},{13,12},{... | collective-permute-start | bytes 4718600 | tf_op jit(solution)/shard_map/ppermute | solution.py:62
  1074.8 7.3 copy-start.1
  1077.0 36.8 %collective-permute-start.6 = (bf16[256,3072]{1,0:T(8,128)(2,1)S(1)}, bf16[256,3072]{1,0:T(8,128)(2,1)S(1)}, u32[]{:S(2)}, u32[]{:S(2)}) collective-permute-start(bf16[256,3072]{1,0:T(8,128)(2,1)S(1)} %get-tuple-element.5), channel_id=1, source_target_pairs={{0,1},{1,2},{2,3},{4,5},{5,6},{6,7},{8,9},{9,10},{10,11},{12,13},{... | collective-permute-start | bytes 4718600 | tf_op jit(solution)/shard_map/ppermute | solution.py:61
  1080.6 67.7 %collective-permute-start.7 = (bf16[256,3072]{1,0:T(8,128)(2,1)S(1)}, bf16[256,3072]{1,0:T(8,128)(2,1)}, u32[]{:S(2)}, u32[]{:S(2)}) collective-permute-start(bf16[256,3072]{1,0:T(8,128)(2,1)S(1)} %get-tuple-element.4), channel_id=1, source_target_pairs={{1,0},{2,1},{3,2},{5,4},{6,5},{7,6},{9,8},{10,9},{11,10},{13,12},{... | collective-permute-start | bytes 4718600 | tf_op jit(solution)/shard_map/ppermute | solution.py:62
Sparse Core Ops, SparseCore 0:
  276.7 633.5 all-gather.4
  1156.5 630.9 all-gather.6
